TPU v7x, 256 devices: a whole 4x4x8 slice. The times are simulated.
256 devices in a mesh: pos: 16 (over x_hi, z), exp: 16 (over y, x_lo, core).
Axes of the slice: x: 4 (x_hi: 2, x_lo: 2; x = x_hi * 2 + x_lo), y: 4, z: 8, core: 2. Of those that a mesh axis runs over, the one named last changes fastest.
Arguments:
- patches: bfloat16 [65536, 4, 256], P(('pos', 'exp')), may hold values from -6 to 6
- conv_weight: bfloat16 [3, 256, 2048], replicated, may hold values from -0.21875 to 0.21875
- phi: bfloat16 [2048, 128], replicated, may hold values from -40 to 40, as said below
- w_in: bfloat16 [16, 2048, 8192], P('exp', None, 'pos'), may hold values from -0.125 to 0.125
- w_out: bfloat16 [16, 8192, 2048], P('exp', 'pos'), may hold values from -0.0625 to 0.0625
Outputs:
- mixed: bfloat16 [65536, 4, 2048], P(('pos', 'exp'))
Inputs may be any that keep to these rules, and one draw needn't show every extreme that they name: phi is real-valued.
All inputs are finite; a program needn't handle non-finite values.
Results may differ from a plain program's by a relative error of at most 0.019.
The roundings to bfloat16 on the way count: a program that leaves them out, or rounds other values in their place, can miss the bound.
Values may be sent and summed in bfloat16 or wider, within the bound.
No kernel may reach another device: no remote copies, remote signals or barrier semaphores. Data moves between devices by JAX's collectives and lax.ppermute only.
A program may use at most 128 MiB of HBM per device.

v0:
```python
import jax
import jax.numpy as jnp
from jax import lax
from jax.sharding import PartitionSpec as P

D = 2048
SLOTS_PER = 8


def with_halo(array, sides, width):
    for axis, dim in sides:
        count, length = (lax.axis_size(axis), array.shape[dim])
        up = [(i, (i + 1) % count) for i in range(count - 1)]
        down = [(j, i) for i, j in up]
        last = lax.slice_in_dim(array, length - width, length, axis=dim)
        initial = lax.slice_in_dim(array, 0, width, axis=dim)
        before = lax.ppermute(last, axis, up)
        after = lax.ppermute(initial, axis, down)
        array = jnp.concatenate([before, array, after], axis=dim)
    return array


def butterfly_sum(value, axis):
    count = lax.axis_size(axis)
    step = 1
    while step < count:
        pairs = [(i, i ^ step) for i in range(count)]
        value = value + lax.ppermute(value, axis, pairs)
        step *= 2
    return value


def merge(mine, theirs):
    peak = jnp.maximum(mine[:, D], theirs[:, D])
    a = jnp.exp(mine[:, D] - peak)[:, None]
    b = jnp.exp(theirs[:, D] - peak)[:, None]
    merged = mine * a + theirs * b
    return merged.at[:, D].set(peak)


def butterfly_softmax_sum(value, axis):
    count = lax.axis_size(axis)
    step = 1
    while step < count:
        pairs = [(i, i ^ step) for i in range(count)]
        value = merge(value, lax.ppermute(value, axis, pairs))
        step *= 2
    return value


def per_device(patches, conv_weight, phi, w_in, w_out):
    channels, periods, samples = patches.shape
    every = ("pos", "exp")
    padded = with_halo(jnp.swapaxes(patches, 0, 1), ((every, 1),), 1)
    window = jnp.concatenate([padded[:, offset : offset + channels] for offset in range(3)], axis=2)
    window = window.reshape(periods * channels, 3 * samples)
    taps = conv_weight.reshape(3 * samples, D)
    flat = jnp.dot(window, taps, preferred_element_type=jnp.float32).astype(jnp.bfloat16)
    logits = jnp.dot(flat, phi, preferred_element_type=jnp.float32)
    slots = logits.shape[1]
    local_peak = jnp.max(logits, axis=0)
    raw_weights = jnp.exp(logits - local_peak)
    local_total = jnp.sum(raw_weights, axis=0)
    every_slot = lax.dot_general(
        raw_weights.astype(jnp.bfloat16),
        flat,
        (((0,), (0,)), ((), ())),
        preferred_element_type=jnp.float32,
    )
    extra = jnp.zeros((slots, 128), jnp.float32)
    extra = extra.at[:, 0].set(local_peak).at[:, 1].set(local_total)
    packed = jnp.concatenate([every_slot, extra], axis=1)
    groups = lax.axis_size("exp")
    mine = lax.all_to_all(packed, "exp", 0, 0, tiled=True).reshape(groups, SLOTS_PER, -1)
    peaks = mine[:, :, D]
    peak = jnp.max(peaks, axis=0)
    scale = jnp.exp(peaks - peak)
    sums = jnp.sum(mine[:, :, :D] * scale[:, :, None], axis=0)
    total = jnp.sum(mine[:, :, D + 1] * scale, axis=0)
    owned = jnp.concatenate(
        [sums, jnp.zeros((SLOTS_PER, 128), jnp.float32).at[:, 0].set(peak).at[:, 1].set(total)],
        axis=1,
    )
    owned = butterfly_softmax_sum(owned, "pos")
    slot_in = (owned[:, :D] / owned[:, D + 1 : D + 2]).astype(jnp.bfloat16)
    hidden = jax.nn.gelu(
        jnp.dot(slot_in, w_in[0], preferred_element_type=jnp.float32), approximate=True
    ).astype(jnp.bfloat16)
    expert_term = jnp.dot(hidden, w_out[0], preferred_element_type=jnp.float32)
    slot_out = butterfly_sum(expert_term, "pos").astype(jnp.bfloat16)
    row_peak = jnp.max(logits, axis=1, keepdims=True)
    row_weights = jnp.exp(logits - row_peak)
    combine = (row_weights / jnp.sum(row_weights, axis=1, keepdims=True)).astype(jnp.bfloat16)
    mixed = jnp.dot(
        combine,
        lax.all_gather(slot_out, "exp", axis=0, tiled=True),
        preferred_element_type=jnp.float32,
    )
    return jnp.swapaxes(mixed.astype(jnp.bfloat16).reshape(periods, channels, D), 0, 1)


def solution(mesh):
    in_specs = (
        P(("pos", "exp"), None, None),
        P(),
        P(),
        P("exp", None, "pos"),
        P("exp", "pos", None),
    )
    out_specs = P(("pos", "exp"), None, None)
    return jax.shard_map(
        per_device, mesh=mesh, in_specs=in_specs, out_specs=out_specs, check_vma=False
    )
```

profile of v0, /device:TPU:1, one launch (start us, length us, event | category | flops | bytes accessed | tf_op | source)
XLA Modules:
  0.0 136.0 jit_solution(183512765969925446)
XLA Ops:
  0.0 1.3 copy.64
  1.3 4.5 %collective-permute-start = (bf16[4,1,256]{2,1,0:T(2,128)(2,1)S(1)}, bf16[4,1,256]{2,1,0:T(2,128)(2,1)S(1)}, u32[]{:S(2)}, u32[]{:S(2)}) collective-permute-start(bf16[4,1,256]{2,1,0:T(2,128)(2,1)S(1)} %get-tuple-element.116), channel_id=1, source_target_pairs={{0,1},{1,2},{2,3},{3,4},{4,5},{5,6},{6,7},{7,8},{8,9},{9,10},{10,1... | collective-permute-start | bytes 6152 | tf_op jit(solution)/shard_map/ppermute | solution.py:17
  5.8 1.9 %collective-permute-start.1 = (bf16[4,1,256]{2,1,0:T(2,128)(2,1)S(1)}, bf16[4,1,256]{2,1,0:T(2,128)(2,1)S(1)}, u32[]{:S(2)}, u32[]{:S(2)}) collective-permute-start(bf16[4,1,256]{2,1,0:T(2,128)(2,1)S(1)} %get-tuple-element.117), channel_id=1, source_target_pairs={{1,0},{2,1},{3,2},{4,3},{5,4},{6,5},{7,6},{8,7},{9,8},{10,9},{11,1... | collective-permute-start | bytes 6152 | tf_op jit(solution)/shard_map/ppermute | solution.py:18
  7.7 0.7 compare_reduce_fusion.2
  9.1 1.6 %collective-permute-done.1 = bf16[4,1,256]{2,1,0:T(2,128)(2,1)S(1)} collective-permute-done((bf16[4,1,256]{2,1,0:T(2,128)(2,1)S(1)}, bf16[4,1,256]{2,1,0:T(2,128)(2,1)S(1)}, u32[]{:S(2)}, u32[]{:S(2)}) %collective-permute-start.1) | collective-permute-done | bytes 2080 | tf_op jit(solution)/shard_map/ppermute | solution.py:18
  11.0 3.6 %convolution_convert_fusion.1 = bf16[1024,2048]{1,0:T(8,128)(2,1)S(1)} fusion(bf16[1024,768]{1,0:T(8,128)(2,1)S(1)} %bitcast.53, bf16[768,2048]{1,0:T(8,128)(2,1)S(1)} %bitcast.49), kind=kOutput, calls=%fused_computation.2 | convolution fusion | flops 3223322624 | bytes 8912896 | tf_op jit(solution)/shard_map/dot_general | solution.py:58
  14.7 1.3 fusion.57
  16.0 1.7 %fusion.10 = f32[128,2048]{1,0:T(8,128)} fusion(bf16[1024,2048]{1,0:T(8,128)(2,1)S(1)} %convolution_convert_fusion.1, f32[1024,128]{1,0:T(8,128)S(1)} %get-tuple-element.118, f32[128]{0:T(128)S(1)} %get-tuple-element.104), kind=kOutput, calls=%fused_computation.21 | convolution fusion | flops 537133056 | bytes 5767680 | tf_op jit(solution)/shard_map/dot_general | solution.py:64
  20.0 1.3 maximum_bitcast_fusion
  21.3 25.0 %all_to_all.9 = f32[16,8,2176]{2,1,0:T(8,128)S(1)} all-to-all(f32[16,8,2176]{2,1,0:T(8,128)S(1)} %maximum_bitcast_fusion), channel_id=1, replica_groups=mesh['pos'=16,'exp'=16] {'exp'}, dimensions={0} | all-to-all | bytes 2228224 | tf_op jit(solution)/shard_map/all_to_all | solution.py:74
  46.4 1.0 copy-done.1
  49.6 1.4 %fusion.6 = f32[8,2048]{1,0:T(8,128)S(1)} fusion(f32[16,8,2176]{2,1,0:T(8,128)} %copy-done.1, f32[16,8]{1,0:T(8,128)S(1)} %copy.53), kind=kLoop, calls=%fused_computation.13 | loop fusion | flops 507904 | bytes 1114624 | tf_op jit(solution)/shard_map/reduce_sum | solution.py:78
  51.0 1.7 %collective-permute-start.2 = (f32[8,2176]{1,0:T(8,128)S(1)}, f32[8,2176]{1,0:T(8,128)S(1)}, u32[]{:S(2)}, u32[]{:S(2)}) collective-permute-start(f32[8,2176]{1,0:T(8,128)S(1)} %pad_maximum_fusion.2), channel_id=1, source_target_pairs={{0,16},{16,0},{32,48},{48,32},{64,80},{80,64},{96,112},{112,96},{1... | collective-permute-start | bytes 208904 | tf_op jit(solution)/shard_map/ppermute | solution.py:46
  53.4 1.4 %collective-permute-done.2 = f32[8,2176]{1,0:T(8,128)S(1)} collective-permute-done((f32[8,2176]{1,0:T(8,128)S(1)}, f32[8,2176]{1,0:T(8,128)S(1)}, u32[]{:S(2)}, u32[]{:S(2)}) %collective-permute-start.2) | collective-permute-done | bytes 69664 | tf_op jit(solution)/shard_map/ppermute | solution.py:46
  55.7 5.6 %collective-permute-start.3 = (f32[8,2176]{1,0:T(8,128)S(1)}, f32[8,2176]{1,0:T(8,128)S(1)}, u32[]{:S(2)}, u32[]{:S(2)}) collective-permute-start(f32[8,2176]{1,0:T(8,128)S(1)} %scatter.30), channel_id=1, source_target_pairs={{0,32},{16,48},{32,0},{48,16},{64,96},{80,112},{96,64},{112,80},{1... | collective-permute-start | bytes 208904 | tf_op jit(solution)/shard_map/ppermute | solution.py:46
  61.3 1.7 %collective-permute-done.3 = f32[8,2176]{1,0:T(8,128)S(1)} collective-permute-done((f32[8,2176]{1,0:T(8,128)S(1)}, f32[8,2176]{1,0:T(8,128)S(1)}, u32[]{:S(2)}, u32[]{:S(2)}) %collective-permute-start.3) | collective-permute-done | bytes 69664 | tf_op jit(solution)/shard_map/ppermute | solution.py:46
  64.0 3.2 %collective-permute-start.4 = (f32[8,2176]{1,0:T(8,128)S(1)}, f32[8,2176]{1,0:T(8,128)S(1)}, u32[]{:S(2)}, u32[]{:S(2)}) collective-permute-start(f32[8,2176]{1,0:T(8,128)S(1)} %scatter.31), channel_id=1, source_target_pairs={{0,64},{16,80},{32,96},{48,112},{64,0},{80,16},{96,32},{112,48},{1... | collective-permute-start | bytes 208904 | tf_op jit(solution)/shard_map/ppermute | solution.py:46
  67.2 4.0 %collective-permute-done.4 = f32[8,2176]{1,0:T(8,128)S(1)} collective-permute-done((f32[8,2176]{1,0:T(8,128)S(1)}, f32[8,2176]{1,0:T(8,128)S(1)}, u32[]{:S(2)}, u32[]{:S(2)}) %collective-permute-start.4) | collective-permute-done | bytes 69664 | tf_op jit(solution)/shard_map/ppermute | solution.py:46
  72.2 2.8 %collective-permute-start.5 = (f32[8,2176]{1,0:T(8,128)S(1)}, f32[8,2176]{1,0:T(8,128)S(1)}, u32[]{:S(2)}, u32[]{:S(2)}) collective-permute-start(f32[8,2176]{1,0:T(8,128)S(1)} %scatter.34), channel_id=1, source_target_pairs={{0,128},{16,144},{32,160},{48,176},{64,192},{80,208},{96,224},{112... | collective-permute-start | bytes 208904 | tf_op jit(solution)/shard_map/ppermute | solution.py:46
  75.0 1.9 %collective-permute-done.5 = f32[8,2176]{1,0:T(8,128)S(1)} collective-permute-done((f32[8,2176]{1,0:T(8,128)S(1)}, f32[8,2176]{1,0:T(8,128)S(1)}, u32[]{:S(2)}, u32[]{:S(2)}) %collective-permute-start.5) | collective-permute-done | bytes 69664 | tf_op jit(solution)/shard_map/ppermute | solution.py:46
  77.4 3.0 %fusion = f32[8,2048]{1,0:T(8,128)S(1)} fusion(bf16[1,512,2048]{2,1,0:T(8,128)(2,1)} %param.25, bf16[1,2048,512]{2,1,0:T(8,128)(2,1)} %param.24, f32[8,2176]{1,0:T(8,128)S(1)} %multiply_add_fusion, f32[8]{0:T(128)S(1)} %slice_reduce_fusion), kind=kOutput, calls=%fused_computation.3 | convolution fusion | flops 33624064 | bytes 4325888 | tf_op jit(solution)/shard_map/dot_general | solution.py:89
  80.4 1.3 collective-permute-start.6
  81.7 1.8 %collective-permute-done.6 = f32[8,2048]{1,0:T(8,128)S(1)} collective-permute-done((f32[8,2048]{1,0:T(8,128)S(1)}, f32[8,2048]{1,0:T(8,128)S(1)}, u32[]{:S(2)}, u32[]{:S(2)}) %collective-permute-start.6) | collective-permute-done | bytes 65568 | tf_op jit(solution)/shard_map/ppermute | solution.py:28
  83.5 2.9 %collective-permute-start.7 = (f32[8,2048]{1,0:T(8,128)S(1)}, f32[8,2048]{1,0:T(8,128)S(1)}, u32[]{:S(2)}, u32[]{:S(2)}) collective-permute-start(f32[8,2048]{1,0:T(8,128)S(1)} %add.60), channel_id=1, source_target_pairs={{0,32},{16,48},{32,0},{48,16},{64,96},{80,112},{96,64},{112,80},{1... | collective-permute-start | bytes 196616 | tf_op jit(solution)/shard_map/ppermute | solution.py:28
  86.4 1.7 %collective-permute-done.7 = f32[8,2048]{1,0:T(8,128)S(1)} collective-permute-done((f32[8,2048]{1,0:T(8,128)S(1)}, f32[8,2048]{1,0:T(8,128)S(1)}, u32[]{:S(2)}, u32[]{:S(2)}) %collective-permute-start.7) | collective-permute-done | bytes 65568 | tf_op jit(solution)/shard_map/ppermute | solution.py:28
  88.1 3.2 %collective-permute-start.8 = (f32[8,2048]{1,0:T(8,128)S(1)}, f32[8,2048]{1,0:T(8,128)S(1)}, u32[]{:S(2)}, u32[]{:S(2)}) collective-permute-start(f32[8,2048]{1,0:T(8,128)S(1)} %add.61), channel_id=1, source_target_pairs={{0,64},{16,80},{32,96},{48,112},{64,0},{80,16},{96,32},{112,48},{1... | collective-permute-start | bytes 196616 | tf_op jit(solution)/shard_map/ppermute | solution.py:28
  91.3 4.3 %collective-permute-done.8 = f32[8,2048]{1,0:T(8,128)S(1)} collective-permute-done((f32[8,2048]{1,0:T(8,128)S(1)}, f32[8,2048]{1,0:T(8,128)S(1)}, u32[]{:S(2)}, u32[]{:S(2)}) %collective-permute-start.8) | collective-permute-done | bytes 65568 | tf_op jit(solution)/shard_map/ppermute | solution.py:28
  95.6 3.7 %collective-permute-start.9 = (f32[8,2048]{1,0:T(8,128)S(1)}, f32[8,2048]{1,0:T(8,128)S(1)}, u32[]{:S(2)}, u32[]{:S(2)}) collective-permute-start(f32[8,2048]{1,0:T(8,128)S(1)} %add.62), channel_id=1, source_target_pairs={{0,128},{16,144},{32,160},{48,176},{64,192},{80,208},{96,224},{112... | collective-permute-start | bytes 196616 | tf_op jit(solution)/shard_map/ppermute | solution.py:28
  99.4 1.7 %collective-permute-done.9 = f32[8,2048]{1,0:T(8,128)S(1)} collective-permute-done((f32[8,2048]{1,0:T(8,128)S(1)}, f32[8,2048]{1,0:T(8,128)S(1)}, u32[]{:S(2)}, u32[]{:S(2)}) %collective-permute-start.9) | collective-permute-done | bytes 65568 | tf_op jit(solution)/shard_map/ppermute | solution.py:28
  101.0 27.4 %all_gather.3 = bf16[128,2048]{1,0:T(8,128)(2,1)S(1)} all-gather(bf16[8,2048]{1,0:T(8,128)(2,1)S(1)} %add_convert_fusion), channel_id=1, replica_groups=mesh['pos'=16,'exp'=16] {'exp'}, dimensions={0}, use_global_device_ids=true | all-gather | bytes 557056 | tf_op jit(solution)/shard_map/all_gather | solution.py:96
  128.4 2.4 %convolution_convert_fusion = bf16[1024,2048]{1,0:T(8,128)(2,1)S(1)} fusion(bf16[128,2048]{1,0:T(8,128)(2,1)S(1)} %all_gather.3, f32[1024,128]{1,0:T(8,128)} %copy-done.2, f32[1024]{0:T(1024)S(1)} %get-tuple-element.101, f32[1024]{0:T(1024)S(1)} %get-tuple-element.103), kind=kOutput, calls=%fused_computation.1 | convolution fusion | flops 539361280 | bytes 5251072 | tf_op jit(solution)/shard_map/dot_general | solution.py:94
  130.8 5.3 %copy.63 = bf16[4,256,2048]{2,0,1:T(4,128)(2,1)} copy(bf16[4,256,2048]{2,1,0:T(8,128)(2,1)S(1)} %bitcast.50) | data formatting | bytes 8388608 | tf_op jit(solution)/shard_map/reshape | solution.py:99
  (51 shorter events, 9.4 us)
Async XLA Ops:
  0.0 11.0 %copy-start = (bf16[3,256,2048]{2,1,0:T(8,128)(2,1)S(1)}, bf16[3,256,2048]{2,1,0:T(8,128)(2,1)}, u32[]{:S(2)}) copy-start(bf16[3,256,2048]{2,1,0:T(8,128)(2,1)} %param.22) | copy-start | bytes 9437188
  1.3 7.8 %collective-permute-start = (bf16[4,1,256]{2,1,0:T(2,128)(2,1)S(1)}, bf16[4,1,256]{2,1,0:T(2,128)(2,1)S(1)}, u32[]{:S(2)}, u32[]{:S(2)}) collective-permute-start(bf16[4,1,256]{2,1,0:T(2,128)(2,1)S(1)} %get-tuple-element.116), channel_id=1, source_target_pairs={{0,1},{1,2},{2,3},{3,4},{4,5},{5,6},{6,7},{7,8},{8,9},{9,10},{10,1... | collective-permute-start | bytes 6152 | tf_op jit(solution)/shard_map/ppermute | solution.py:17
  5.8 4.9 %collective-permute-start.1 = (bf16[4,1,256]{2,1,0:T(2,128)(2,1)S(1)}, bf16[4,1,256]{2,1,0:T(2,128)(2,1)S(1)}, u32[]{:S(2)}, u32[]{:S(2)}) collective-permute-start(bf16[4,1,256]{2,1,0:T(2,128)(2,1)S(1)} %get-tuple-element.117), channel_id=1, source_target_pairs={{1,0},{2,1},{3,2},{4,3},{5,4},{6,5},{7,6},{8,7},{9,8},{10,9},{11,1... | collective-permute-start | bytes 6152 | tf_op jit(solution)/shard_map/ppermute | solution.py:18
  11.0 3.7 %copy-start.3 = (bf16[2048,128]{1,0:T(8,128)(2,1)S(1)}, bf16[2048,128]{1,0:T(8,128)(2,1)}, u32[]{:S(2)}) copy-start(bf16[2048,128]{1,0:T(8,128)(2,1)} %param.23) | copy-start | bytes 1572868
  16.0 2.8 %copy-start.2 = (f32[1024,128]{1,0:T(8,128)}, f32[1024,128]{1,0:T(8,128)S(1)}, u32[]{:S(2)}) copy-start(f32[1024,128]{1,0:T(8,128)S(1)} %get-tuple-element.118) | copy-start | bytes 1572868
  46.4 1.0 copy-start.1
  51.0 3.7 %collective-permute-start.2 = (f32[8,2176]{1,0:T(8,128)S(1)}, f32[8,2176]{1,0:T(8,128)S(1)}, u32[]{:S(2)}, u32[]{:S(2)}) collective-permute-start(f32[8,2176]{1,0:T(8,128)S(1)} %pad_maximum_fusion.2), channel_id=1, source_target_pairs={{0,16},{16,0},{32,48},{48,32},{64,80},{80,64},{96,112},{112,96},{1... | collective-permute-start | bytes 208904 | tf_op jit(solution)/shard_map/ppermute | solution.py:46
  55.7 7.3 %collective-permute-start.3 = (f32[8,2176]{1,0:T(8,128)S(1)}, f32[8,2176]{1,0:T(8,128)S(1)}, u32[]{:S(2)}, u32[]{:S(2)}) collective-permute-start(f32[8,2176]{1,0:T(8,128)S(1)} %scatter.30), channel_id=1, source_target_pairs={{0,32},{16,48},{32,0},{48,16},{64,96},{80,112},{96,64},{112,80},{1... | collective-permute-start | bytes 208904 | tf_op jit(solution)/shard_map/ppermute | solution.py:46
  64.0 7.2 %collective-permute-start.4 = (f32[8,2176]{1,0:T(8,128)S(1)}, f32[8,2176]{1,0:T(8,128)S(1)}, u32[]{:S(2)}, u32[]{:S(2)}) collective-permute-start(f32[8,2176]{1,0:T(8,128)S(1)} %scatter.31), channel_id=1, source_target_pairs={{0,64},{16,80},{32,96},{48,112},{64,0},{80,16},{96,32},{112,48},{1... | collective-permute-start | bytes 208904 | tf_op jit(solution)/shard_map/ppermute | solution.py:46
  72.2 4.8 %collective-permute-start.5 = (f32[8,2176]{1,0:T(8,128)S(1)}, f32[8,2176]{1,0:T(8,128)S(1)}, u32[]{:S(2)}, u32[]{:S(2)}) collective-permute-start(f32[8,2176]{1,0:T(8,128)S(1)} %scatter.34), channel_id=1, source_target_pairs={{0,128},{16,144},{32,160},{48,176},{64,192},{80,208},{96,224},{112... | collective-permute-start | bytes 208904 | tf_op jit(solution)/shard_map/ppermute | solution.py:46
  80.4 3.1 %collective-permute-start.6 = (f32[8,2048]{1,0:T(8,128)S(1)}, f32[8,2048]{1,0:T(8,128)S(1)}, u32[]{:S(2)}, u32[]{:S(2)}) collective-permute-start(f32[8,2048]{1,0:T(8,128)S(1)} %fusion), channel_id=1, source_target_pairs={{0,16},{16,0},{32,48},{48,32},{64,80},{80,64},{96,112},{112,96},{1... | collective-permute-start | bytes 196616 | tf_op jit(solution)/shard_map/ppermute | solution.py:28
  83.5 4.6 %collective-permute-start.7 = (f32[8,2048]{1,0:T(8,128)S(1)}, f32[8,2048]{1,0:T(8,128)S(1)}, u32[]{:S(2)}, u32[]{:S(2)}) collective-permute-start(f32[8,2048]{1,0:T(8,128)S(1)} %add.60), channel_id=1, source_target_pairs={{0,32},{16,48},{32,0},{48,16},{64,96},{80,112},{96,64},{112,80},{1... | collective-permute-start | bytes 196616 | tf_op jit(solution)/shard_map/ppermute | solution.py:28
  88.1 7.5 %collective-permute-start.8 = (f32[8,2048]{1,0:T(8,128)S(1)}, f32[8,2048]{1,0:T(8,128)S(1)}, u32[]{:S(2)}, u32[]{:S(2)}) collective-permute-start(f32[8,2048]{1,0:T(8,128)S(1)} %add.61), channel_id=1, source_target_pairs={{0,64},{16,80},{32,96},{48,112},{64,0},{80,16},{96,32},{112,48},{1... | collective-permute-start | bytes 196616 | tf_op jit(solution)/shard_map/ppermute | solution.py:28
  95.6 5.4 %collective-permute-start.9 = (f32[8,2048]{1,0:T(8,128)S(1)}, f32[8,2048]{1,0:T(8,128)S(1)}, u32[]{:S(2)}, u32[]{:S(2)}) collective-permute-start(f32[8,2048]{1,0:T(8,128)S(1)} %add.62), channel_id=1, source_target_pairs={{0,128},{16,144},{32,160},{48,176},{64,192},{80,208},{96,224},{112... | collective-permute-start | bytes 196616 | tf_op jit(solution)/shard_map/ppermute | solution.py:28
where the time goes:
time: 136 us
  blocking collectives  52.4 us (39%)
  starting transfers between devices  30.9 us (23%)
  waiting for transfers between devices  20.1 us (15%)
  matrix products  12.1 us (9%)
  other arithmetic  11.2 us (8%)
  local copies, waits for them, and re-layouts  9.09 us (7%)
    all_gather x1, blocking collectives, per_device(): lax.all_gather(slot_out, 'exp', axis=0, tiled=True)  27.4 us
    all_to_all x1, blocking collectives, per_device(): lax.all_to_all(packed, 'exp', 0, 0, tiled=True)  25 us
    ppermute x4, starting transfers between devices, butterfly_softmax_sum(): value = merge(value, lax.ppermute(value, axis, pairs))  13.4 us
    ppermute x4, starting transfers between devices, butterfly_sum(): value = value + lax.ppermute(value, axis, pairs)  11.1 us
    ppermute x4, waiting for transfers between devices, butterfly_sum(): value = value + lax.ppermute(value, axis, pairs)  9.47 us
    ppermute x4, waiting for transfers between devices, butterfly_softmax_sum(): value = merge(value, lax.ppermute(value, axis, pairs))  8.97 us
    reshape x1, local copies, waits for them, and re-layouts, per_device(): mixed.astype(jnp.bfloat16).reshape(periods, channels, D)  5.25 us
    another operation x7, other arithmetic  4.53 us
  transfers between devices with their start and end apart: 10, of which 9 were waited for; matrix products, arithmetic and copies ran while one was open for 1% of the time, Pallas kernels for 0%

commit v1 on v0

--- a/solution.py
+++ b/solution.py
@@ -91,11 +91,16 @@
     row_peak = jnp.max(logits, axis=1, keepdims=True)
     row_weights = jnp.exp(logits - row_peak)
     combine = (row_weights / jnp.sum(row_weights, axis=1, keepdims=True)).astype(jnp.bfloat16)
-    mixed = jnp.dot(
-        combine,
-        lax.all_gather(slot_out, "exp", axis=0, tiled=True),
-        preferred_element_type=jnp.float32,
+    arrays_store = lambda body: jnp.concatenate(
+        lax.all_to_all(
+            jnp.stack([body for _ in range(lax.psum(1, axis_name="exp"))]),
+            concat_axis=0,
+            axis_name="exp",
+            split_axis=0,
+        ),
+        axis=0,
     )
+    mixed = jnp.dot(combine, arrays_store(slot_out), preferred_element_type=jnp.float32)
     return jnp.swapaxes(mixed.astype(jnp.bfloat16).reshape(periods, channels, D), 0, 1)
 
 

time: 136 us -> 130 us (0.956)
  blocking collectives: 52.4 us -> 45.3 us
    all_gather x1 -> x0, blocking collectives: 27.4 us -> none  [per_device(): lax.all_gather(slot_out, 'exp', axis=0, tiled=True)]
    all_to_all x0 -> x1, blocking collectives: none -> 20.3 us  [per_device(): lax.all_to_all(jnp.stack([body for _ in range(lax.psum(1, axis_name='exp'...]
  transfers between devices with their start and end apart: 10 -> 10, of which waited for: 9 -> 9; matrix products, arithmetic and copies ran while one was open for 1% -> 2% of each run, Pallas kernels for 0% -> 0%
where the time goes in v1:
time: 130 us; the launch traced here: 129 us
  blocking collectives  45.3 us (35%)
  starting transfers between devices  30.9 us (24%)
  waiting for transfers between devices  20.1 us (15%)
  matrix products  12.1 us (9%)
  other arithmetic  11.2 us (9%)
  local copies, waits for them, and re-layouts  9.13 us (7%)
    all_to_all x1, blocking collectives, per_device(): lax.all_to_all(packed, 'exp', 0, 0, tiled=True)  25 us
    all_to_all x1, blocking collectives, per_device(): lax.all_to_all(jnp.stack([body for _ in range(lax.psum(1, axis_name='exp'...  20.3 us
    ppermute x4, starting transfers between devices, butterfly_softmax_sum(): value = merge(value, lax.ppermute(value, axis, pairs))  13.4 us
    ppermute x4, starting transfers between devices, butterfly_sum(): value = value + lax.ppermute(value, axis, pairs)  11.1 us
    ppermute x4, waiting for transfers between devices, butterfly_sum(): value = value + lax.ppermute(value, axis, pairs)  9.47 us
    ppermute x4, waiting for transfers between devices, butterfly_softmax_sum(): value = merge(value, lax.ppermute(value, axis, pairs))  8.97 us
    reshape x1, local copies, waits for them, and re-layouts, per_device(): mixed.astype(jnp.bfloat16).reshape(periods, channels, D)  5.25 us
    another operation x7, other arithmetic  4.53 us
  transfers between devices with their start and end apart: 10, of which 9 were waited for; matrix products, arithmetic and copies ran while one was open for 2% of the time, Pallas kernels for 0%

profile of v1, /device:TPU:1, one launch (start us, length us, event | category | flops | bytes accessed | tf_op | source)
XLA Modules:
  0.0 129.0 jit_solution(14427451472551880548)
XLA Ops:
  0.0 1.3 copy.64
  1.3 4.5 %collective-permute-start = (bf16[4,1,256]{2,1,0:T(2,128)(2,1)S(1)}, bf16[4,1,256]{2,1,0:T(2,128)(2,1)S(1)}, u32[]{:S(2)}, u32[]{:S(2)}) collective-permute-start(bf16[4,1,256]{2,1,0:T(2,128)(2,1)S(1)} %get-tuple-element.116), channel_id=1, source_target_pairs={{0,1},{1,2},{2,3},{3,4},{4,5},{5,6},{6,7},{7,8},{8,9},{9,10},{10,1... | collective-permute-start | bytes 6152 | tf_op jit(solution)/shard_map/ppermute | solution.py:17
  5.8 1.9 %collective-permute-start.1 = (bf16[4,1,256]{2,1,0:T(2,128)(2,1)S(1)}, bf16[4,1,256]{2,1,0:T(2,128)(2,1)S(1)}, u32[]{:S(2)}, u32[]{:S(2)}) collective-permute-start(bf16[4,1,256]{2,1,0:T(2,128)(2,1)S(1)} %get-tuple-element.117), channel_id=1, source_target_pairs={{1,0},{2,1},{3,2},{4,3},{5,4},{6,5},{7,6},{8,7},{9,8},{10,9},{11,1... | collective-permute-start | bytes 6152 | tf_op jit(solution)/shard_map/ppermute | solution.py:18
  7.7 0.7 compare_reduce_fusion.2
  9.1 1.6 %collective-permute-done.1 = bf16[4,1,256]{2,1,0:T(2,128)(2,1)S(1)} collective-permute-done((bf16[4,1,256]{2,1,0:T(2,128)(2,1)S(1)}, bf16[4,1,256]{2,1,0:T(2,128)(2,1)S(1)}, u32[]{:S(2)}, u32[]{:S(2)}) %collective-permute-start.1) | collective-permute-done | bytes 2080 | tf_op jit(solution)/shard_map/ppermute | solution.py:18
  11.0 3.6 %convolution_convert_fusion.1 = bf16[1024,2048]{1,0:T(8,128)(2,1)S(1)} fusion(bf16[1024,768]{1,0:T(8,128)(2,1)S(1)} %bitcast.55, bf16[768,2048]{1,0:T(8,128)(2,1)S(1)} %bitcast.51), kind=kOutput, calls=%fused_computation.2 | convolution fusion | flops 3223322624 | bytes 8912896 | tf_op jit(solution)/shard_map/dot_general | solution.py:58
  14.7 1.3 %fusion.58 = (f32[1024]{0:T(1024)S(1)}, f32[128]{0:T(128)S(1)}, f32[1024,128]{1,0:T(8,128)S(1)}) fusion(bf16[1024,2048]{1,0:T(8,128)(2,1)S(1)} %convolution_convert_fusion.1, bf16[2048,128]{1,0:T(8,128)(2,1)S(1)} %copy-done.3), kind=kOutput, calls=%fused_computation.89 | convolution fusion | flops 537131904 | bytes 5247488 | tf_op jit(solution)/shard_map/dot_general | solution.py:59
  16.0 1.7 %fusion.11 = f32[128,2048]{1,0:T(8,128)} fusion(bf16[1024,2048]{1,0:T(8,128)(2,1)S(1)} %convolution_convert_fusion.1, f32[1024,128]{1,0:T(8,128)S(1)} %get-tuple-element.118, f32[128]{0:T(128)S(1)} %get-tuple-element.104), kind=kOutput, calls=%fused_computation.22 | convolution fusion | flops 537133056 | bytes 5767680 | tf_op jit(solution)/shard_map/dot_general | solution.py:64
  20.0 1.3 %maximum_bitcast_fusion = f32[16,8,2176]{2,1,0:T(8,128)S(1)} fusion(f32[128,128]{1,0:T(8,128)S(1)} %scatter.25, f32[128,2048]{1,0:T(8,128)} %fusion.11), kind=kLoop, calls=%fused_computation.11 | loop fusion | flops 278528 | bytes 2228224 | tf_op jit(solution)/shard_map/all_to_all | solution.py:74
  21.3 25.0 %all_to_all.14 = f32[16,8,2176]{2,1,0:T(8,128)S(1)} all-to-all(f32[16,8,2176]{2,1,0:T(8,128)S(1)} %maximum_bitcast_fusion), channel_id=1, replica_groups=mesh['pos'=16,'exp'=16] {'exp'}, dimensions={0} | all-to-all | bytes 2228224 | tf_op jit(solution)/shard_map/all_to_all | solution.py:74
  46.4 1.0 copy-done.1
  49.6 1.4 %fusion.6 = f32[8,2048]{1,0:T(8,128)S(1)} fusion(f32[16,8,2176]{2,1,0:T(8,128)} %copy-done.1, f32[16,8]{1,0:T(8,128)S(1)} %copy.53), kind=kLoop, calls=%fused_computation.13 | loop fusion | flops 507904 | bytes 1114624 | tf_op jit(solution)/shard_map/reduce_sum | solution.py:78
  51.0 1.7 %collective-permute-start.2 = (f32[8,2176]{1,0:T(8,128)S(1)}, f32[8,2176]{1,0:T(8,128)S(1)}, u32[]{:S(2)}, u32[]{:S(2)}) collective-permute-start(f32[8,2176]{1,0:T(8,128)S(1)} %pad_maximum_fusion.2), channel_id=1, source_target_pairs={{0,16},{16,0},{32,48},{48,32},{64,80},{80,64},{96,112},{112,96},{1... | collective-permute-start | bytes 208904 | tf_op jit(solution)/shard_map/ppermute | solution.py:46
  53.4 1.4 %collective-permute-done.2 = f32[8,2176]{1,0:T(8,128)S(1)} collective-permute-done((f32[8,2176]{1,0:T(8,128)S(1)}, f32[8,2176]{1,0:T(8,128)S(1)}, u32[]{:S(2)}, u32[]{:S(2)}) %collective-permute-start.2) | collective-permute-done | bytes 69664 | tf_op jit(solution)/shard_map/ppermute | solution.py:46
  55.7 5.6 %collective-permute-start.3 = (f32[8,2176]{1,0:T(8,128)S(1)}, f32[8,2176]{1,0:T(8,128)S(1)}, u32[]{:S(2)}, u32[]{:S(2)}) collective-permute-start(f32[8,2176]{1,0:T(8,128)S(1)} %scatter.30), channel_id=1, source_target_pairs={{0,32},{16,48},{32,0},{48,16},{64,96},{80,112},{96,64},{112,80},{1... | collective-permute-start | bytes 208904 | tf_op jit(solution)/shard_map/ppermute | solution.py:46
  61.3 1.7 %collective-permute-done.3 = f32[8,2176]{1,0:T(8,128)S(1)} collective-permute-done((f32[8,2176]{1,0:T(8,128)S(1)}, f32[8,2176]{1,0:T(8,128)S(1)}, u32[]{:S(2)}, u32[]{:S(2)}) %collective-permute-start.3) | collective-permute-done | bytes 69664 | tf_op jit(solution)/shard_map/ppermute | solution.py:46
  64.0 3.2 %collective-permute-start.4 = (f32[8,2176]{1,0:T(8,128)S(1)}, f32[8,2176]{1,0:T(8,128)S(1)}, u32[]{:S(2)}, u32[]{:S(2)}) collective-permute-start(f32[8,2176]{1,0:T(8,128)S(1)} %scatter.31), channel_id=1, source_target_pairs={{0,64},{16,80},{32,96},{48,112},{64,0},{80,16},{96,32},{112,48},{1... | collective-permute-start | bytes 208904 | tf_op jit(solution)/shard_map/ppermute | solution.py:46
  67.2 4.0 %collective-permute-done.4 = f32[8,2176]{1,0:T(8,128)S(1)} collective-permute-done((f32[8,2176]{1,0:T(8,128)S(1)}, f32[8,2176]{1,0:T(8,128)S(1)}, u32[]{:S(2)}, u32[]{:S(2)}) %collective-permute-start.4) | collective-permute-done | bytes 69664 | tf_op jit(solution)/shard_map/ppermute | solution.py:46
  72.2 2.8 %collective-permute-start.5 = (f32[8,2176]{1,0:T(8,128)S(1)}, f32[8,2176]{1,0:T(8,128)S(1)}, u32[]{:S(2)}, u32[]{:S(2)}) collective-permute-start(f32[8,2176]{1,0:T(8,128)S(1)} %scatter.34), channel_id=1, source_target_pairs={{0,128},{16,144},{32,160},{48,176},{64,192},{80,208},{96,224},{112... | collective-permute-start | bytes 208904 | tf_op jit(solution)/shard_map/ppermute | solution.py:46
  75.0 1.9 %collective-permute-done.5 = f32[8,2176]{1,0:T(8,128)S(1)} collective-permute-done((f32[8,2176]{1,0:T(8,128)S(1)}, f32[8,2176]{1,0:T(8,128)S(1)}, u32[]{:S(2)}, u32[]{:S(2)}) %collective-permute-start.5) | collective-permute-done | bytes 69664 | tf_op jit(solution)/shard_map/ppermute | solution.py:46
  77.4 3.0 %fusion = f32[8,2048]{1,0:T(8,128)S(1)} fusion(bf16[1,512,2048]{2,1,0:T(8,128)(2,1)} %param.25, bf16[1,2048,512]{2,1,0:T(8,128)(2,1)} %param.24, f32[8,2176]{1,0:T(8,128)S(1)} %multiply_add_fusion, f32[8]{0:T(128)S(1)} %slice_reduce_fusion), kind=kOutput, calls=%fused_computation.3 | convolution fusion | flops 33624064 | bytes 4325888 | tf_op jit(solution)/shard_map/dot_general | solution.py:89
  80.4 1.3 %collective-permute-start.6 = (f32[8,2048]{1,0:T(8,128)S(1)}, f32[8,2048]{1,0:T(8,128)S(1)}, u32[]{:S(2)}, u32[]{:S(2)}) collective-permute-start(f32[8,2048]{1,0:T(8,128)S(1)} %fusion), channel_id=1, source_target_pairs={{0,16},{16,0},{32,48},{48,32},{64,80},{80,64},{96,112},{112,96},{1... | collective-permute-start | bytes 196616 | tf_op jit(solution)/shard_map/ppermute | solution.py:28
  81.7 1.8 %collective-permute-done.6 = f32[8,2048]{1,0:T(8,128)S(1)} collective-permute-done((f32[8,2048]{1,0:T(8,128)S(1)}, f32[8,2048]{1,0:T(8,128)S(1)}, u32[]{:S(2)}, u32[]{:S(2)}) %collective-permute-start.6) | collective-permute-done | bytes 65568 | tf_op jit(solution)/shard_map/ppermute | solution.py:28
  83.5 2.9 %collective-permute-start.7 = (f32[8,2048]{1,0:T(8,128)S(1)}, f32[8,2048]{1,0:T(8,128)S(1)}, u32[]{:S(2)}, u32[]{:S(2)}) collective-permute-start(f32[8,2048]{1,0:T(8,128)S(1)} %add.60), channel_id=1, source_target_pairs={{0,32},{16,48},{32,0},{48,16},{64,96},{80,112},{96,64},{112,80},{1... | collective-permute-start | bytes 196616 | tf_op jit(solution)/shard_map/ppermute | solution.py:28
  86.4 1.7 %collective-permute-done.7 = f32[8,2048]{1,0:T(8,128)S(1)} collective-permute-done((f32[8,2048]{1,0:T(8,128)S(1)}, f32[8,2048]{1,0:T(8,128)S(1)}, u32[]{:S(2)}, u32[]{:S(2)}) %collective-permute-start.7) | collective-permute-done | bytes 65568 | tf_op jit(solution)/shard_map/ppermute | solution.py:28
  88.1 3.2 %collective-permute-start.8 = (f32[8,2048]{1,0:T(8,128)S(1)}, f32[8,2048]{1,0:T(8,128)S(1)}, u32[]{:S(2)}, u32[]{:S(2)}) collective-permute-start(f32[8,2048]{1,0:T(8,128)S(1)} %add.61), channel_id=1, source_target_pairs={{0,64},{16,80},{32,96},{48,112},{64,0},{80,16},{96,32},{112,48},{1... | collective-permute-start | bytes 196616 | tf_op jit(solution)/shard_map/ppermute | solution.py:28
  91.3 4.3 %collective-permute-done.8 = f32[8,2048]{1,0:T(8,128)S(1)} collective-permute-done((f32[8,2048]{1,0:T(8,128)S(1)}, f32[8,2048]{1,0:T(8,128)S(1)}, u32[]{:S(2)}, u32[]{:S(2)}) %collective-permute-start.8) | collective-permute-done | bytes 65568 | tf_op jit(solution)/shard_map/ppermute | solution.py:28
  95.6 3.7 %collective-permute-start.9 = (f32[8,2048]{1,0:T(8,128)S(1)}, f32[8,2048]{1,0:T(8,128)S(1)}, u32[]{:S(2)}, u32[]{:S(2)}) collective-permute-start(f32[8,2048]{1,0:T(8,128)S(1)} %add.62), channel_id=1, source_target_pairs={{0,128},{16,144},{32,160},{48,176},{64,192},{80,208},{96,224},{112... | collective-permute-start | bytes 196616 | tf_op jit(solution)/shard_map/ppermute | solution.py:28
  99.4 1.7 %collective-permute-done.9 = f32[8,2048]{1,0:T(8,128)S(1)} collective-permute-done((f32[8,2048]{1,0:T(8,128)S(1)}, f32[8,2048]{1,0:T(8,128)S(1)}, u32[]{:S(2)}, u32[]{:S(2)}) %collective-permute-start.9) | collective-permute-done | bytes 65568 | tf_op jit(solution)/shard_map/ppermute | solution.py:28
  101.1 20.3 %all_to_all.15 = bf16[16,8,2048]{2,1,0:T(8,128)(2,1)S(1)} all-to-all(bf16[16,8,2048]{2,1,0:T(8,128)(2,1)S(1)} %stack.2), channel_id=1, replica_groups=mesh['pos'=16,'exp'=16] {'exp'}, dimensions={0} | all-to-all | bytes 1048576 | tf_op jit(solution)/shard_map/all_to_all | solution.py:95
  121.4 2.4 %convolution_convert_fusion = bf16[1024,2048]{1,0:T(8,128)(2,1)S(1)} fusion(bf16[16,8,2048]{2,1,0:T(8,128)(2,1)S(1)} %all_to_all.15, f32[1024,128]{1,0:T(8,128)} %copy-done.2, f32[1024]{0:T(1024)S(1)} %get-tuple-element.101, f32[1024]{0:T(1024)S(1)} %get-tuple-element.103), kind=kOutput, calls=%fused_computation.1 | convolution fusion | flops 539361280 | bytes 5251072 | tf_op jit(solution)/shard_map/dot_general | solution.py:103
  123.7 5.3 %copy.63 = bf16[4,256,2048]{2,0,1:T(4,128)(2,1)} copy(bf16[4,256,2048]{2,1,0:T(8,128)(2,1)S(1)} %bitcast.52) | data formatting | bytes 8388608 | tf_op jit(solution)/shard_map/reshape | solution.py:104
  (52 shorter events, 9.4 us)
Async XLA Ops:
  0.0 11.0 %copy-start = (bf16[3,256,2048]{2,1,0:T(8,128)(2,1)S(1)}, bf16[3,256,2048]{2,1,0:T(8,128)(2,1)}, u32[]{:S(2)}) copy-start(bf16[3,256,2048]{2,1,0:T(8,128)(2,1)} %param.22) | copy-start | bytes 9437188
  1.3 7.8 %collective-permute-start = (bf16[4,1,256]{2,1,0:T(2,128)(2,1)S(1)}, bf16[4,1,256]{2,1,0:T(2,128)(2,1)S(1)}, u32[]{:S(2)}, u32[]{:S(2)}) collective-permute-start(bf16[4,1,256]{2,1,0:T(2,128)(2,1)S(1)} %get-tuple-element.116), channel_id=1, source_target_pairs={{0,1},{1,2},{2,3},{3,4},{4,5},{5,6},{6,7},{7,8},{8,9},{9,10},{10,1... | collective-permute-start | bytes 6152 | tf_op jit(solution)/shard_map/ppermute | solution.py:17
  5.8 4.9 %collective-permute-start.1 = (bf16[4,1,256]{2,1,0:T(2,128)(2,1)S(1)}, bf16[4,1,256]{2,1,0:T(2,128)(2,1)S(1)}, u32[]{:S(2)}, u32[]{:S(2)}) collective-permute-start(bf16[4,1,256]{2,1,0:T(2,128)(2,1)S(1)} %get-tuple-element.117), channel_id=1, source_target_pairs={{1,0},{2,1},{3,2},{4,3},{5,4},{6,5},{7,6},{8,7},{9,8},{10,9},{11,1... | collective-permute-start | bytes 6152 | tf_op jit(solution)/shard_map/ppermute | solution.py:18
  11.0 3.7 %copy-start.3 = (bf16[2048,128]{1,0:T(8,128)(2,1)S(1)}, bf16[2048,128]{1,0:T(8,128)(2,1)}, u32[]{:S(2)}) copy-start(bf16[2048,128]{1,0:T(8,128)(2,1)} %param.23) | copy-start | bytes 1572868
  16.0 2.8 %copy-start.2 = (f32[1024,128]{1,0:T(8,128)}, f32[1024,128]{1,0:T(8,128)S(1)}, u32[]{:S(2)}) copy-start(f32[1024,128]{1,0:T(8,128)S(1)} %get-tuple-element.118) | copy-start | bytes 1572868
  46.4 1.0 copy-start.1
  51.0 3.7 %collective-permute-start.2 = (f32[8,2176]{1,0:T(8,128)S(1)}, f32[8,2176]{1,0:T(8,128)S(1)}, u32[]{:S(2)}, u32[]{:S(2)}) collective-permute-start(f32[8,2176]{1,0:T(8,128)S(1)} %pad_maximum_fusion.2), channel_id=1, source_target_pairs={{0,16},{16,0},{32,48},{48,32},{64,80},{80,64},{96,112},{112,96},{1... | collective-permute-start | bytes 208904 | tf_op jit(solution)/shard_map/ppermute | solution.py:46
  55.7 7.3 %collective-permute-start.3 = (f32[8,2176]{1,0:T(8,128)S(1)}, f32[8,2176]{1,0:T(8,128)S(1)}, u32[]{:S(2)}, u32[]{:S(2)}) collective-permute-start(f32[8,2176]{1,0:T(8,128)S(1)} %scatter.30), channel_id=1, source_target_pairs={{0,32},{16,48},{32,0},{48,16},{64,96},{80,112},{96,64},{112,80},{1... | collective-permute-start | bytes 208904 | tf_op jit(solution)/shard_map/ppermute | solution.py:46
  64.0 7.2 %collective-permute-start.4 = (f32[8,2176]{1,0:T(8,128)S(1)}, f32[8,2176]{1,0:T(8,128)S(1)}, u32[]{:S(2)}, u32[]{:S(2)}) collective-permute-start(f32[8,2176]{1,0:T(8,128)S(1)} %scatter.31), channel_id=1, source_target_pairs={{0,64},{16,80},{32,96},{48,112},{64,0},{80,16},{96,32},{112,48},{1... | collective-permute-start | bytes 208904 | tf_op jit(solution)/shard_map/ppermute | solution.py:46
  72.2 4.8 %collective-permute-start.5 = (f32[8,2176]{1,0:T(8,128)S(1)}, f32[8,2176]{1,0:T(8,128)S(1)}, u32[]{:S(2)}, u32[]{:S(2)}) collective-permute-start(f32[8,2176]{1,0:T(8,128)S(1)} %scatter.34), channel_id=1, source_target_pairs={{0,128},{16,144},{32,160},{48,176},{64,192},{80,208},{96,224},{112... | collective-permute-start | bytes 208904 | tf_op jit(solution)/shard_map/ppermute | solution.py:46
  80.4 3.1 %collective-permute-start.6 = (f32[8,2048]{1,0:T(8,128)S(1)}, f32[8,2048]{1,0:T(8,128)S(1)}, u32[]{:S(2)}, u32[]{:S(2)}) collective-permute-start(f32[8,2048]{1,0:T(8,128)S(1)} %fusion), channel_id=1, source_target_pairs={{0,16},{16,0},{32,48},{48,32},{64,80},{80,64},{96,112},{112,96},{1... | collective-permute-start | bytes 196616 | tf_op jit(solution)/shard_map/ppermute | solution.py:28
  83.5 4.6 %collective-permute-start.7 = (f32[8,2048]{1,0:T(8,128)S(1)}, f32[8,2048]{1,0:T(8,128)S(1)}, u32[]{:S(2)}, u32[]{:S(2)}) collective-permute-start(f32[8,2048]{1,0:T(8,128)S(1)} %add.60), channel_id=1, source_target_pairs={{0,32},{16,48},{32,0},{48,16},{64,96},{80,112},{96,64},{112,80},{1... | collective-permute-start | bytes 196616 | tf_op jit(solution)/shard_map/ppermute | solution.py:28
  88.1 7.5 %collective-permute-start.8 = (f32[8,2048]{1,0:T(8,128)S(1)}, f32[8,2048]{1,0:T(8,128)S(1)}, u32[]{:S(2)}, u32[]{:S(2)}) collective-permute-start(f32[8,2048]{1,0:T(8,128)S(1)} %add.61), channel_id=1, source_target_pairs={{0,64},{16,80},{32,96},{48,112},{64,0},{80,16},{96,32},{112,48},{1... | collective-permute-start | bytes 196616 | tf_op jit(solution)/shard_map/ppermute | solution.py:28
  95.6 5.4 %collective-permute-start.9 = (f32[8,2048]{1,0:T(8,128)S(1)}, f32[8,2048]{1,0:T(8,128)S(1)}, u32[]{:S(2)}, u32[]{:S(2)}) collective-permute-start(f32[8,2048]{1,0:T(8,128)S(1)} %add.62), channel_id=1, source_target_pairs={{0,128},{16,144},{32,160},{48,176},{64,192},{80,208},{96,224},{112... | collective-permute-start | bytes 196616 | tf_op jit(solution)/shard_map/ppermute | solution.py:28
